TPU v7x, 32 devices: a whole 2x2x4 slice. The times are simulated.
32 devices in a mesh: grp: 8 (over z, x), leaf: 4 (over y, core).
Axes of the slice: x: 2, y: 2, z: 4, core: 2. Of those that a mesh axis runs over, the one named last changes fastest.
Arguments:
- inputs: float32 [65536, 64], P(('grp', 'leaf')), may hold values from -6 to 6
- freqs: float32 [64, 256], replicated, may hold values from -0.75 to 0.75
- phases: float32 [256], replicated, may hold values from -3.140625 to 3.140625
- sample_weight: float32 [65536], P(('grp', 'leaf')), as said below
- stored: float32 [32, 256, 256], P(('grp', 'leaf')), as said below
- root: int32 [32], replicated, may hold values from 0 to 31, each once
Outputs:
- factor: float32 [256, 256], replicated
- basis: float32 [65536, 256], P(('grp', 'leaf'))
Inputs may be any that keep to these rules, and one draw needn't show every extreme that they name: `root`: each device index once, in the order grp first, leaf second; only the first entry is read. `stored`: each slot is upper triangular with a positive diagonal. `sample_weight`: positive row weights.
All inputs are finite; a program needn't handle non-finite values.
Results may differ from a plain program's by a relative error of at most 0.0003.
Values sent between devices are 32-bit elements; how exact they have to be, the bound alone decides.
No kernel may reach another device: no remote copies, remote signals or barrier semaphores. Data moves between devices by JAX's collectives and lax.ppermute only.
A program may use at most 64 MiB of HBM per device.

v0:
```python
import math
import jax
import jax.numpy as jnp
from jax import lax
from jax.sharding import PartitionSpec as P


def partner(array, axis, distance):
    return lax.ppermute(array, axis, [(i, i ^ 1 << distance) for i in range(lax.axis_size(axis))])


def spread(array, axis, root):
    mine = lax.axis_index(axis) == root
    return lax.psum(jnp.where(mine, array, jnp.zeros_like(array)), axis)


def per_device(inputs, freqs, phases, sample_weight, stored, root):
    total_rows = inputs.shape[0] * lax.axis_size("grp") * lax.axis_size("leaf")
    norm_scale = 1.0 / math.sqrt(total_rows)
    proj = jnp.dot(inputs, freqs, precision=lax.Precision.HIGHEST) + phases[None, :]
    features = jnp.sqrt(sample_weight)[:, None] * jnp.cos(proj) * norm_scale
    gram = lax.dot_general(
        features, features, (((0,), (0,)), ((), ())), precision=lax.Precision.HIGHEST
    )
    running = stored[0]
    payload = gram
    for bit_leaf in range(lax.axis_size("leaf").bit_length() - 1):
        payload = payload + partner(payload, "leaf", bit_leaf)
    for bit_grp in range(lax.axis_size("grp").bit_length() - 1):
        payload = payload + partner(payload, "grp", bit_grp)
    gram = payload
    carried = spread(running, ("grp", "leaf"), root[0])
    gram = jnp.dot(carried.T, carried, precision=lax.Precision.HIGHEST) + gram
    lower = jnp.linalg.cholesky(gram)
    solved = jax.scipy.linalg.solve_triangular(lower, features.T, lower=True)
    basis = solved.T * math.sqrt(total_rows)
    return (lower.T, basis)


def solution(mesh):
    return jax.shard_map(
        per_device,
        mesh=mesh,
        in_specs=(
            P(("grp", "leaf"), None),
            P(),
            P(),
            P(("grp", "leaf")),
            P(("grp", "leaf"), None, None),
            P(),
        ),
        out_specs=(P(), P(("grp", "leaf"), None)),
        check_vma=False,
    )
```

profile of v0, /device:TPU:0, one launch (start us, length us, event | category | flops | bytes accessed | tf_op | source)
XLA Modules:
  0.0 246.1 jit_solution(17475438517466494014)
XLA Ops:
  7.2 0.0 copy-start
  7.2 0.0 all-reduce.3.cloned.1.call-start
  7.2 0.8 sqrt.3
  8.0 0.3 copy-done
  8.2 9.5 %fusion.2 = f32[2048,256]{1,0:T(8,128)S(1)} fusion(f32[2048,64]{0,1:T(8,128)S(1)} %copy-done, f32[64,256]{1,0:T(8,128)} %param.7, f32[256]{0:T(256)} %param.8, f32[2048]{0:T(1024)S(1)} %sqrt.3), kind=kOutput, calls=%fused_computation.5 | convolution fusion | flops 404226048 | bytes 2696192 | tf_op jit(solution)/shard_map/dot_general | solution.py:20
  17.8 3.6 %fusion.16 = f32[256,256]{0,1:T(8,128)S(1)} fusion(f32[2048,256]{1,0:T(8,128)S(1)} %fusion.2), kind=kOutput, calls=%fused_computation.39 | convolution fusion | flops 1610612736 | bytes 2359296 | tf_op jit(solution)/shard_map/dot_general | solution.py:22
  21.4 0.0 copy-start.2
  21.4 0.0 copy-start.1
  21.4 0.6 collective-permute-start
  22.0 1.2 collective-permute-done
  23.2 2.9 %collective-permute-start.1 = (f32[256,256]{0,1:T(8,128)S(1)}, f32[256,256]{0,1:T(8,128)S(1)}, u32[]{:S(2)}, u32[]{:S(2)}) collective-permute-start(f32[256,256]{0,1:T(8,128)S(1)} %add.59), channel_id=1, source_target_pairs={{0,2},{1,3},{2,0},{3,1},{4,6},{5,7},{6,4},{7,5},{8,10},{9,11},{10,... | collective-permute-start | bytes 786440 | tf_op jit(solution)/shard_map/ppermute | solution.py:9
  26.1 6.6 %collective-permute-done.1 = f32[256,256]{0,1:T(8,128)S(1)} collective-permute-done((f32[256,256]{0,1:T(8,128)S(1)}, f32[256,256]{0,1:T(8,128)S(1)}, u32[]{:S(2)}, u32[]{:S(2)}) %collective-permute-start.1) | collective-permute-done | bytes 262176 | tf_op jit(solution)/shard_map/ppermute | solution.py:9
  32.8 1.8 collective-permute-start.2
  34.6 6.1 %collective-permute-done.2 = f32[256,256]{0,1:T(8,128)S(1)} collective-permute-done((f32[256,256]{0,1:T(8,128)S(1)}, f32[256,256]{0,1:T(8,128)S(1)}, u32[]{:S(2)}, u32[]{:S(2)}) %collective-permute-start.2) | collective-permute-done | bytes 262176 | tf_op jit(solution)/shard_map/ppermute | solution.py:9
  40.6 1.6 collective-permute-start.3
  42.2 0.0 copy-done.2
  42.3 0.0 copy-done.1
  42.3 0.7 select_bitcast_fusion
  43.0 0.0 all-reduce.3.cloned.1.call-update
  43.0 4.6 %collective-permute-done.3 = f32[256,256]{0,1:T(8,128)S(1)} collective-permute-done((f32[256,256]{0,1:T(8,128)S(1)}, f32[256,256]{0,1:T(8,128)S(1)}, u32[]{:S(2)}, u32[]{:S(2)}) %collective-permute-start.3) | collective-permute-done | bytes 262176 | tf_op jit(solution)/shard_map/ppermute | solution.py:9
  47.7 2.3 collective-permute-start.4
  50.0 121.1 %all-reduce.3.cloned.1.call-done = f32[256,256]{1,0:T(8,128)} async-done(((f32[256,256]{1,0:T(8,128)}), f32[256,256]{1,0:T(8,128)}) %all-reduce.3.cloned.1.call-update) | async-done | bytes 262160 | tf_op jit(solution)/shard_map/psum | solution.py:14
  171.1 1.6 fusion.15
  172.7 0.0 collective-permute-done.4
  172.7 0.1 add_add_fusion
  172.8 0.1 copy.11
  173.0 11.7 %cholesky.49 = f32[128,128]{1,0:T(8,128)S(1)} custom-call(f32[128,128]{1,0:T(8,128)S(1)} %cholesky.115), custom_call_target="Cholesky" | custom-call | tf_op jit(solution)/shard_map/jit(cholesky)/cholesky | solution.py:34
  184.7 9.8 %custom-call.15 = f32[1,128,128]{1,2,0:T(8,128)S(1)} custom-call(f32[1,128,128]{2,1,0:T(8,128)S(1)} %get-tuple-element.27), custom_call_target="InvertDiagBlocksLowerTriangular" | custom-call | tf_op jit(solution)/shard_map/jit(cholesky)/cholesky | solution.py:34
  194.6 0.2 constant_dynamic-update-slice_fusion.1
  194.8 0.3 convolution_subtract_fusion.1
  195.1 11.7 %cholesky.103 = f32[128,128]{1,0:T(8,128)S(1)} custom-call(f32[128,128]{1,0:T(8,128)S(1)} %convolution_subtract_fusion.1), custom_call_target="Cholesky" | custom-call | tf_op jit(solution)/shard_map/jit(cholesky)/cholesky | solution.py:34
  206.8 0.6 compare_reduce_fusion
  208.8 0.8 copy.12
  209.6 0.1 triangular_solve.42
  209.7 3.9 %while.1 = (s32[]{:T(128)}, f32[256,256]{1,0:T(8,128)S(1)}, s32[2,2]{1,0:T(2,128)S(1)}, f32[2,128,128]{2,1,0:T(8,128)S(1)}, s32[]{:T(128)}) while((s32[]{:T(128)}, f32[256,256]{1,0:T(8,128)S(1)}, s32[2,2]{1,0:T(2,128)S(1)}, f32[2,128,128]{2,1,0:T(8,128)S(1)}, s32[]{:T(128)}) %tuple.29), condition=%wide.while_cond, body=%wide.while_body.sunk | while | flops 2 | bytes 131189 | solution.py:35
  209.7 0.6 fusion.28
  210.3 1.3 bitcast_dynamic-update-slice_fusion.2
  211.7 0.6 fusion.28
  212.3 1.3 bitcast_dynamic-update-slice_fusion.2
  213.6 19.7 %custom-call.16 = f32[2,128,128]{1,2,0:T(8,128)S(1)} custom-call(f32[2,128,128]{2,1,0:T(8,128)S(1)} %get-tuple-element.9), custom_call_target="InvertDiagBlocksLowerTriangular" | custom-call | tf_op jit(solution)/shard_map/jit(_solve_triangular)/triangular_solve | solution.py:35
  233.3 1.1 fusion.4
  234.4 1.8 convolution_subtract_fusion
  236.2 1.1 fusion.10
  237.3 0.2 fusion.3
  237.5 1.8 copy.13
  (14 shorter events, 0.3 us)
Async XLA Ops:
  7.2 1.1 copy-start
  7.2 163.9 %all-reduce.3.cloned.1.call-start = ((), (), s32[]{:S(2)}) async-start(), calls=%async_computation | async-start | bytes 524288 | tf_op jit(solution)/shard_map/psum | solution.py:14
  21.4 20.8 %copy-start.2 = (s32[32]{0:T(128)S(1)}, s32[32]{0:T(128)}, u32[]{:S(2)}) copy-start(s32[32]{0:T(128)} %param.11) | copy-start | bytes 388
  21.4 20.9 %copy-start.1 = (f32[1,256,256]{2,1,0:T(8,128)S(1)}, f32[1,256,256]{2,1,0:T(8,128)}, u32[]{:S(2)}) copy-start(f32[1,256,256]{2,1,0:T(8,128)} %param.10) | copy-start | bytes 786436
  21.4 1.7 collective-permute-start
  23.2 9.5 %collective-permute-start.1 = (f32[256,256]{0,1:T(8,128)S(1)}, f32[256,256]{0,1:T(8,128)S(1)}, u32[]{:S(2)}, u32[]{:S(2)}) collective-permute-start(f32[256,256]{0,1:T(8,128)S(1)} %add.59), channel_id=1, source_target_pairs={{0,2},{1,3},{2,0},{3,1},{4,6},{5,7},{6,4},{7,5},{8,10},{9,11},{10,... | collective-permute-start | bytes 786440 | tf_op jit(solution)/shard_map/ppermute | solution.py:9
  32.8 7.8 %collective-permute-start.2 = (f32[256,256]{0,1:T(8,128)S(1)}, f32[256,256]{0,1:T(8,128)S(1)}, u32[]{:S(2)}, u32[]{:S(2)}) collective-permute-start(f32[256,256]{0,1:T(8,128)S(1)} %add.60), channel_id=1, source_target_pairs={{0,4},{4,0},{8,12},{12,8},{16,20},{20,16},{24,28},{28,24},{1,5},{5... | collective-permute-start | bytes 786440 | tf_op jit(solution)/shard_map/ppermute | solution.py:9
  40.6 7.0 %collective-permute-start.3 = (f32[256,256]{0,1:T(8,128)S(1)}, f32[256,256]{0,1:T(8,128)S(1)}, u32[]{:S(2)}, u32[]{:S(2)}) collective-permute-start(f32[256,256]{0,1:T(8,128)S(1)} %add.61), channel_id=1, source_target_pairs={{0,8},{4,12},{8,0},{12,4},{16,24},{20,28},{24,16},{28,20},{1,9},{5... | collective-permute-start | bytes 786440 | tf_op jit(solution)/shard_map/ppermute | solution.py:9
  47.7 125.1 %collective-permute-start.4 = (f32[256,256]{0,1:T(8,128)S(1)}, f32[256,256]{0,1:T(8,128)S(1)}, u32[]{:S(2)}, u32[]{:S(2)}) collective-permute-start(f32[256,256]{0,1:T(8,128)S(1)} %add.62), channel_id=1, source_target_pairs={{0,16},{4,20},{8,24},{12,28},{16,0},{20,4},{24,8},{28,12},{1,17},{... | collective-permute-start | bytes 786440 | tf_op jit(solution)/shard_map/ppermute | solution.py:9
Sparse Core Ops, SparseCore 0:
  43.2 127.8 all-reduce.2
where the time goes:
time: 246 us
  waiting for transfers between devices  140 us (57%)
  other arithmetic  54.8 us (22%)
  matrix products  19.2 us (8%)
  between operations  15.6 us (6%)
  starting transfers between devices  9.21 us (4%)
  local copies, waits for them, and re-layouts  7.77 us (3%)
    psum x1, waiting for transfers between devices, spread(): return lax.psum(jnp.where(mine, array, jnp.zeros_like(array)), axis)  121 us
    another operation x6, other arithmetic, per_device(): lower = jnp.linalg.cholesky(gram)  34 us
    another operation x3, other arithmetic, per_device(): solved = jax.scipy.linalg.solve_triangular(lower, features.T, lower=True)  19.7 us
    ppermute x5, waiting for transfers between devices, partner(): lax.ppermute(array, axis, [(i, i ^ 1 << distance) for i in range(lax.axis...  18.4 us
    dot_general x1, matrix products, per_device(): jnp.dot(inputs, freqs, precision=lax.Precision.HIGHEST) + phases[None, :]  9.54 us
    ppermute x5, starting transfers between devices, partner(): lax.ppermute(array, axis, [(i, i ^ 1 << distance) for i in range(lax.axis...  9.17 us
  transfers between devices with their start and end apart: 6, of which 5 were waited for; matrix products, arithmetic and copies ran while one was open for 1% of the time, Pallas kernels for 0%

commit v1 on v0

--- a/solution.py
+++ b/solution.py
@@ -3,6 +3,7 @@
 import jax.numpy as jnp
 from jax import lax
 from jax.sharding import PartitionSpec as P
+from jax.lax import all_gather
 
 
 def partner(array, axis, distance):
@@ -11,7 +12,7 @@
 
 def spread(array, axis, root):
     mine = lax.axis_index(axis) == root
-    return lax.psum(jnp.where(mine, array, jnp.zeros_like(array)), axis)
+    return jnp.sum(all_gather(jnp.where(mine, array, jnp.zeros_like(array)), axis), 0)
 
 
 def per_device(inputs, freqs, phases, sample_weight, stored, root):

time: 246 us -> 176 us (0.72)
  waiting for transfers between devices: 140 us -> 64.5 us
  other arithmetic: 54.8 us -> 58.9 us
    psum x1 -> x0, waiting for transfers between devices: 121 us -> none  [spread(): return lax.psum(jnp.where(mine, array, jnp.zeros_like(array)), axis)]
    all_gather x0 -> x1, waiting for transfers between devices: none -> 37.4 us  [spread(): all_gather(jnp.where(mine, array, jnp.zeros_like(array)), axis)]
    ppermute x5, waiting for transfers between devices: 18.4 us -> 27.1 us  [partner(): lax.ppermute(array, axis, [(i, i ^ 1 << distance) for i in range(lax.axis...]
    reduce_sum x0 -> x1, other arithmetic: none -> 3.93 us  [spread(): jnp.sum(all_gather(jnp.where(mine, array, jnp.zeros_like(array)), axis), 0)]
  transfers between devices with their start and end apart: 6 -> 6, of which waited for: 5 -> 5; matrix products, arithmetic and copies ran while one was open for 1% -> 11% of each run, Pallas kernels for 0% -> 0%
where the time goes in v1:
time: 176 us; the launch traced here: 175 us
  waiting for transfers between devices  64.5 us (37%)
  other arithmetic  58.9 us (33%)
  matrix products  18.2 us (10%)
  between operations  16.2 us (9%)
  starting transfers between devices  9.96 us (6%)
  local copies, waits for them, and re-layouts  7.52 us (4%)
    all_gather x1, waiting for transfers between devices, spread(): all_gather(jnp.where(mine, array, jnp.zeros_like(array)), axis)  37.4 us
    another operation x6, other arithmetic, per_device(): lower = jnp.linalg.cholesky(gram)  34.1 us
    ppermute x5, waiting for transfers between devices, partner(): lax.ppermute(array, axis, [(i, i ^ 1 << distance) for i in range(lax.axis...  27.1 us
    another operation x3, other arithmetic, per_device(): solved = jax.scipy.linalg.solve_triangular(lower, features.T, lower=True)  19.7 us
    ppermute x5, starting transfers between devices, partner(): lax.ppermute(array, axis, [(i, i ^ 1 << distance) for i in range(lax.axis...  9.92 us
    dot_general x1, matrix products, per_device(): jnp.dot(inputs, freqs, precision=lax.Precision.HIGHEST) + phases[None, :]  9.55 us
    another operation x3, matrix products, per_device(): solved = jax.scipy.linalg.solve_triangular(lower, features.T, lower=True)  3.96 us
    another operation x6, local copies, waits for them, and re-layouts  3.93 us
  transfers between devices with their start and end apart: 6, of which 5 were waited for; matrix products, arithmetic and copies ran while one was open for 11% of the time, Pallas kernels for 0%

profile of v1, /device:TPU:0, one launch (start us, length us, event | category | flops | bytes accessed | tf_op | source)
XLA Modules:
  0.0 175.3 jit_solution(15486323896641178968)
XLA Ops:
  7.2 0.0 copy-start
  7.2 0.0 all-gather.2.cloned.1.call-start
  7.9 0.7 broadcast_select_fusion
  8.7 0.0 all-gather.2.cloned.1.call-update
  8.7 0.7 sqrt.3
  9.4 0.0 copy-done
  9.4 9.5 %fusion.2 = f32[2048,256]{1,0:T(8,128)S(1)} fusion(f32[2048,64]{0,1:T(8,128)S(1)} %copy-done, f32[64,256]{1,0:T(8,128)} %param.7, f32[256]{0:T(256)} %param.8, f32[2048]{0:T(1024)S(1)} %sqrt.3), kind=kOutput, calls=%fused_computation.5 | convolution fusion | flops 404226048 | bytes 2696192 | tf_op jit(solution)/shard_map/dot_general | solution.py:21
  18.9 3.6 %fusion.16 = f32[256,256]{0,1:T(8,128)S(1)} fusion(f32[2048,256]{1,0:T(8,128)S(1)} %fusion.2), kind=kOutput, calls=%fused_computation.39 | convolution fusion | flops 1610612736 | bytes 2359296 | tf_op jit(solution)/shard_map/dot_general | solution.py:23
  22.6 0.6 collective-permute-start
  23.1 1.2 collective-permute-done
  24.3 2.9 %collective-permute-start.1 = (f32[256,256]{0,1:T(8,128)S(1)}, f32[256,256]{0,1:T(8,128)S(1)}, u32[]{:S(2)}, u32[]{:S(2)}) collective-permute-start(f32[256,256]{0,1:T(8,128)S(1)} %add.57), channel_id=1, source_target_pairs={{0,2},{1,3},{2,0},{3,1},{4,6},{5,7},{6,4},{7,5},{8,10},{9,11},{10,... | collective-permute-start | bytes 786440 | tf_op jit(solution)/shard_map/ppermute | solution.py:10
  27.3 6.6 %collective-permute-done.1 = f32[256,256]{0,1:T(8,128)S(1)} collective-permute-done((f32[256,256]{0,1:T(8,128)S(1)}, f32[256,256]{0,1:T(8,128)S(1)}, u32[]{:S(2)}, u32[]{:S(2)}) %collective-permute-start.1) | collective-permute-done | bytes 262176 | tf_op jit(solution)/shard_map/ppermute | solution.py:10
  33.9 1.8 %collective-permute-start.2 = (f32[256,256]{0,1:T(8,128)S(1)}, f32[256,256]{0,1:T(8,128)S(1)}, u32[]{:S(2)}, u32[]{:S(2)}) collective-permute-start(f32[256,256]{0,1:T(8,128)S(1)} %add.58), channel_id=1, source_target_pairs={{0,4},{4,0},{8,12},{12,8},{16,20},{20,16},{24,28},{28,24},{1,5},{5... | collective-permute-start | bytes 786440 | tf_op jit(solution)/shard_map/ppermute | solution.py:10
  35.7 6.1 %collective-permute-done.2 = f32[256,256]{0,1:T(8,128)S(1)} collective-permute-done((f32[256,256]{0,1:T(8,128)S(1)}, f32[256,256]{0,1:T(8,128)S(1)}, u32[]{:S(2)}, u32[]{:S(2)}) %collective-permute-start.2) | collective-permute-done | bytes 262176 | tf_op jit(solution)/shard_map/ppermute | solution.py:10
  41.8 3.1 %collective-permute-start.3 = (f32[256,256]{0,1:T(8,128)S(1)}, f32[256,256]{0,1:T(8,128)S(1)}, u32[]{:S(2)}, u32[]{:S(2)}) collective-permute-start(f32[256,256]{0,1:T(8,128)S(1)} %add.59), channel_id=1, source_target_pairs={{0,8},{4,12},{8,0},{12,4},{16,24},{20,28},{24,16},{28,20},{1,9},{5... | collective-permute-start | bytes 786440 | tf_op jit(solution)/shard_map/ppermute | solution.py:10
  44.9 13.3 %collective-permute-done.3 = f32[256,256]{0,1:T(8,128)S(1)} collective-permute-done((f32[256,256]{0,1:T(8,128)S(1)}, f32[256,256]{0,1:T(8,128)S(1)}, u32[]{:S(2)}, u32[]{:S(2)}) %collective-permute-start.3) | collective-permute-done | bytes 262176 | tf_op jit(solution)/shard_map/ppermute | solution.py:10
  58.2 1.5 collective-permute-start.4
  59.7 37.4 %all-gather.2.cloned.1.call-done = f32[32,256,256]{2,1,0:T(8,128)} async-done(((f32[1,256,256]{2,1,0:T(8,128)}), f32[32,256,256]{2,1,0:T(8,128)}) %all-gather.2.cloned.1.call-update) | async-done | bytes 8388624 | tf_op jit(solution)/shard_map/all_gather | solution.py:15
  97.1 3.9 %reduce_sum.9 = f32[256,256]{1,0:T(8,128)S(1)} reduce(f32[32,256,256]{2,1,0:T(8,128)} %all-gather.2.cloned.1.call-done, f32[]{:T(128)} %constant.89.clone.1), dimensions={0}, to_apply=%region_0.1 | reduce | flops 2031616 | bytes 8650756 | tf_op jit(solution)/shard_map/reduce_sum | solution.py:15
  101.0 0.6 fusion.15
  101.6 0.0 collective-permute-done.4
  101.7 0.1 add_add_fusion
  101.7 0.1 copy.17
  101.9 11.7 %cholesky.49 = f32[128,128]{1,0:T(8,128)S(1)} custom-call(f32[128,128]{1,0:T(8,128)S(1)} %cholesky.115), custom_call_target="Cholesky" | custom-call | tf_op jit(solution)/shard_map/jit(cholesky)/cholesky | solution.py:35
  113.7 9.8 %custom-call.15 = f32[1,128,128]{1,2,0:T(8,128)S(1)} custom-call(f32[1,128,128]{2,1,0:T(8,128)S(1)} %get-tuple-element.29), custom_call_target="InvertDiagBlocksLowerTriangular" | custom-call | tf_op jit(solution)/shard_map/jit(cholesky)/cholesky | solution.py:35
  123.5 0.2 constant_dynamic-update-slice_fusion.1
  123.7 0.3 convolution_subtract_fusion.1
  124.0 11.9 %cholesky.103 = f32[128,128]{1,0:T(8,128)S(1)} custom-call(f32[128,128]{1,0:T(8,128)S(1)} %convolution_subtract_fusion.1), custom_call_target="Cholesky" | custom-call | tf_op jit(solution)/shard_map/jit(cholesky)/cholesky | solution.py:35
  135.9 0.6 compare_reduce_fusion
  137.9 0.8 copy.18
  138.7 0.1 triangular_solve.42
  138.8 4.0 %while.1 = (s32[]{:T(128)}, f32[256,256]{1,0:T(8,128)S(1)}, s32[2,2]{1,0:T(2,128)S(1)}, f32[2,128,128]{2,1,0:T(8,128)S(1)}, s32[]{:T(128)}) while((s32[]{:T(128)}, f32[256,256]{1,0:T(8,128)S(1)}, s32[2,2]{1,0:T(2,128)S(1)}, f32[2,128,128]{2,1,0:T(8,128)S(1)}, s32[]{:T(128)}) %tuple.30), condition=%wide.while_cond, body=%wide.while_body.sunk | while | flops 2 | bytes 131189 | solution.py:36
  138.8 0.6 fusion.28
  139.4 1.4 bitcast_dynamic-update-slice_fusion.2
  140.8 0.6 fusion.28
  141.4 1.4 bitcast_dynamic-update-slice_fusion.2
  142.8 19.7 %custom-call.16 = f32[2,128,128]{1,2,0:T(8,128)S(1)} custom-call(f32[2,128,128]{2,1,0:T(8,128)S(1)} %get-tuple-element.9), custom_call_target="InvertDiagBlocksLowerTriangular" | custom-call | tf_op jit(solution)/shard_map/jit(_solve_triangular)/triangular_solve | solution.py:36
  162.5 1.1 fusion.4
  163.5 1.8 %convolution_subtract_fusion = f32[128,2048]{0,1:T(8,128)S(1)} fusion(f32[128,2048]{1,0:T(8,128)S(1)} %fusion.4, f32[256,2048]{0,1:T(8,128)S(1)} %bitcast.45, f32[256,256]{1,0:T(8,128)S(1)} %get-tuple-element.80), kind=kOutput, calls=%fused_computation.6 | convolution fusion | flops 402915328 | bytes 3211264 | tf_op jit(solution)/shard_map/jit(_solve_triangular)/triangular_solve | solution.py:36
  165.4 1.1 fusion.10
  166.4 0.2 fusion.3
  166.6 1.8 %copy.19 = f32[2048,256]{1,0:T(8,128)} copy(f32[2048,256]{0,1:T(8,128)S(1)} %fusion.3) | data formatting | bytes 4194304
  (14 shorter events, 0.3 us)
Async XLA Ops:
  7.2 2.2 %copy-start = (f32[2048,64]{0,1:T(8,128)S(1)}, f32[2048,64]{0,1:T(8,128)}, u32[]{:S(2)}) copy-start(f32[2048,64]{0,1:T(8,128)} %param.6) | copy-start | bytes 1572868
  7.2 89.9 %all-gather.2.cloned.1.call-start = ((), (), s32[]{:S(2)}) async-start(), calls=%async_computation | async-start | bytes 8650752 | tf_op jit(solution)/shard_map/all_gather | solution.py:15
  22.6 1.7 collective-permute-start
  24.3 9.6 %collective-permute-start.1 = (f32[256,256]{0,1:T(8,128)S(1)}, f32[256,256]{0,1:T(8,128)S(1)}, u32[]{:S(2)}, u32[]{:S(2)}) collective-permute-start(f32[256,256]{0,1:T(8,128)S(1)} %add.57), channel_id=1, source_target_pairs={{0,2},{1,3},{2,0},{3,1},{4,6},{5,7},{6,4},{7,5},{8,10},{9,11},{10,... | collective-permute-start | bytes 786440 | tf_op jit(solution)/shard_map/ppermute | solution.py:10
  33.9 7.8 %collective-permute-start.2 = (f32[256,256]{0,1:T(8,128)S(1)}, f32[256,256]{0,1:T(8,128)S(1)}, u32[]{:S(2)}, u32[]{:S(2)}) collective-permute-start(f32[256,256]{0,1:T(8,128)S(1)} %add.58), channel_id=1, source_target_pairs={{0,4},{4,0},{8,12},{12,8},{16,20},{20,16},{24,28},{28,24},{1,5},{5... | collective-permute-start | bytes 786440 | tf_op jit(solution)/shard_map/ppermute | solution.py:10
  41.8 16.4 %collective-permute-start.3 = (f32[256,256]{0,1:T(8,128)S(1)}, f32[256,256]{0,1:T(8,128)S(1)}, u32[]{:S(2)}, u32[]{:S(2)}) collective-permute-start(f32[256,256]{0,1:T(8,128)S(1)} %add.59), channel_id=1, source_target_pairs={{0,8},{4,12},{8,0},{12,4},{16,24},{20,28},{24,16},{28,20},{1,9},{5... | collective-permute-start | bytes 786440 | tf_op jit(solution)/shard_map/ppermute | solution.py:10
  58.2 43.4 %collective-permute-start.4 = (f32[256,256]{0,1:T(8,128)S(1)}, f32[256,256]{0,1:T(8,128)S(1)}, u32[]{:S(2)}, u32[]{:S(2)}) collective-permute-start(f32[256,256]{0,1:T(8,128)S(1)} %add.60), channel_id=1, source_target_pairs={{0,16},{4,20},{8,24},{12,28},{16,0},{20,4},{24,8},{28,12},{1,17},{... | collective-permute-start | bytes 786440 | tf_op jit(solution)/shard_map/ppermute | solution.py:10
Sparse Core Ops, SparseCore 0:
  11.4 85.6 all-gather.1
